TPU v7x, 256 devices: a whole 4x4x8 slice. The times are simulated.
256 devices in a mesh: seq: 64 (over y, z, core), head: 4 (over x).
Axes of the slice: x: 4, y: 4, z: 8, core: 2. Of those that a mesh axis runs over, the one named last changes fastest.
Arguments:
- queries: bfloat16 [32768, 4096], P(('seq', 'head')), may hold values from -6 to 6
- keys: bfloat16 [32768, 4096], P(('seq', 'head')), may hold values from -6 to 6
- values: bfloat16 [32768, 4096], P(('seq', 'head')), may hold values from -6 to 6
- cluster_ids: int32 [32, 32768, 1], P(None, 'seq'), may hold values from 0 to 127; in each aligned block of 128 rows (0 to 127, 128 to 255, ..., all dimensions but the last counted through in order) at most 2 rows name the same one
- out_weight: bfloat16 [4096, 4096], P('head', 'seq'), may hold values from -0.09375 to 0.09375
Outputs:
- projected: bfloat16 [32768, 4096], P('seq', 'head')
Inputs may be any that keep to these rules, and one draw needn't show every extreme that they name: `cluster_ids`: in each aligned block of 128 tokens of one head (the rows of one device), no cluster id appears more than 2 times, and some cluster appears exactly 2 times.
All inputs are finite; a program needn't handle non-finite values.
Results may differ from a plain program's by a relative error of at most 0.014.
Values may be sent and summed in bfloat16 or wider, within the bound.
No kernel may reach another device: no remote copies, remote signals or barrier semaphores. Data moves between devices by JAX's collectives and lax.ppermute only.
A program may use at most 128 MiB of HBM per device.

v0:
```python
import jax
import jax.numpy as jnp
from jax import lax
from jax.sharding import PartitionSpec as P

HEADS = 32
HD = 128
CLUSTERS = 128


def slot_table(block_ids, slot_depth):
    sub_rows = block_ids.shape[-1]
    onehot = (block_ids[..., None] == jnp.arange(CLUSTERS, dtype=jnp.int32)).astype(jnp.float32)
    lower = (jnp.arange(sub_rows)[:, None] >= jnp.arange(sub_rows)[None, :]).astype(jnp.float32)
    running = jnp.einsum("ts,abse->abte", lower, onehot)
    ranking = (jnp.sum(running * onehot, axis=-1) - 1.0).astype(jnp.int32)
    depth_hit = (ranking[..., None] == jnp.arange(slot_depth, dtype=jnp.int32)).astype(jnp.bfloat16)
    return onehot.astype(jnp.bfloat16)[..., :, None] * depth_hit[..., None, :]


def attend_blocks(packed, validity):
    scores = jnp.einsum(
        "cqd,ckd->cqk", packed[0], packed[1], preferred_element_type=jnp.float32
    ) * HD ** (-0.5)
    scores = jnp.where(validity[:, None, :], scores, -1e30)
    row_max = jnp.max(scores, axis=-1, keepdims=True)
    raised = jnp.exp(scores - row_max)
    weights = (raised / jnp.sum(raised, axis=-1, keepdims=True)).astype(jnp.bfloat16)
    return jnp.einsum(
        "cqk,ckd->cqd", weights, packed[2], preferred_element_type=jnp.float32
    ).astype(jnp.bfloat16)


def body(queries, keys, values, cluster_ids, out_weight):
    n_seq = lax.axis_size("seq")
    n_head = lax.axis_size("head")
    head_group = lax.axis_index("head")
    tok_dev = cluster_ids.shape[1]
    sub_rows = tok_dev // n_head
    group_heads = HEADS // n_head
    slot_depth = max(2, 2 * tok_dev // (n_head * CLUSTERS))
    per_owner = group_heads * CLUSTERS // n_seq
    n_src = n_seq * n_head
    all_ids = cluster_ids[:, :, 0]
    own_ids = lax.dynamic_slice_in_dim(all_ids, head_group * sub_rows, sub_rows, 1)
    own_table = slot_table(own_ids[:, None, :], slot_depth)[:, 0]
    stacked = jnp.stack([t.reshape(sub_rows, HEADS, HD) for t in (queries, keys, values)])
    packed = jnp.einsum(
        "htcr,xthd->xhcrd", own_table, stacked, preferred_element_type=jnp.float32
    ).astype(jnp.bfloat16)
    packed = packed.reshape(3, n_head, per_owner, n_seq, slot_depth, HD)
    packed = packed.transpose(0, 3, 1, 2, 4, 5).reshape(3, n_src, per_owner, slot_depth, HD)
    arrived = lax.all_to_all(packed, ("seq", "head"), split_axis=1, concat_axis=1, tiled=True)
    arrived = arrived.transpose(0, 2, 1, 3, 4).reshape(3, per_owner, n_src * slot_depth, HD)
    group_ids = lax.dynamic_slice_in_dim(all_ids, head_group * group_heads, group_heads, 0)
    seen_ids = lax.all_gather(group_ids, "seq", axis=1, tiled=True)
    seen_ids = seen_ids.reshape(group_heads, n_src, sub_rows)
    owned = jnp.arange(CLUSTERS // n_seq, dtype=jnp.int32) * n_seq + lax.axis_index("seq")
    counts = jnp.sum(
        (seen_ids[:, None, :, :] == owned[None, :, None, None]).astype(jnp.int32), axis=-1
    )
    counts = counts.reshape(per_owner, n_src)
    valid = counts[:, :, None] > jnp.arange(slot_depth, dtype=jnp.int32)
    valid = valid.reshape(per_owner, n_src * slot_depth)
    result_block = attend_blocks(arrived, valid)
    result_block = result_block.reshape(per_owner, n_seq, n_head * slot_depth, HD)
    returned = lax.all_to_all(result_block, "seq", split_axis=1, concat_axis=1, tiled=True)
    returned = returned.reshape(group_heads, CLUSTERS, n_head, slot_depth, HD)
    group_ids = group_ids.reshape(group_heads, n_head, sub_rows)
    home_table = slot_table(group_ids, slot_depth)
    gathered = jnp.einsum(
        "hltcr,hclrd->lthd", home_table, returned, preferred_element_type=jnp.float32
    ).astype(jnp.bfloat16)
    gathered = gathered.reshape(tok_dev, group_heads * HD)
    partial_value = jnp.dot(
        gathered,
        lax.all_gather(out_weight, "seq", axis=1, tiled=True),
        preferred_element_type=jnp.float32,
    )
    return lax.psum_scatter(
        partial_value.astype(jnp.bfloat16), "head", scatter_dimension=1, tiled=True
    )


def solution(mesh):
    in_specs = (
        P(("seq", "head"), None),
        P(("seq", "head"), None),
        P(("seq", "head"), None),
        P(None, "seq", None),
        P("head", "seq"),
    )
    out_specs = P("seq", "head")
    return jax.shard_map(body, mesh=mesh, in_specs=in_specs, out_specs=out_specs, check_vma=False)
```

profile of v0, /device:TPU:1, one launch (start us, length us, event | category | flops | bytes accessed | tf_op | source)
XLA Modules:
  0.0 354.4 jit_solution(14528924154040969133)
XLA Ops:
  10.1 1.3 copy.70
  12.1 1.3 copy.71
  15.4 3.3 convert_bitcast_fusion
  18.7 2.6 copy.73
  21.3 4.0 %copy.74 = bf16[3,64,4,16,2,128]{5,3,4,2,1,0:T(8,128)(2,1)S(1)} copy(bf16[3,64,4,16,2,128]{5,1,3,2,4,0:T(8,128)(2,1)S(1)} %bitcast.66) | data formatting | bytes 12582912 | tf_op jit(solution)/shard_map/transpose | solution.py:52
  25.4 3.7 %copy.75 = bf16[3,256,16,2,128]{4,2,3,0,1:T(8,128)(2,1)} copy(bf16[3,256,16,2,128]{4,2,3,1,0:T(8,128)(2,1)S(1)} %bitcast.67) | data formatting | bytes 12582912 | tf_op jit(solution)/shard_map/reshape | solution.py:52
  29.1 16.5 %all-to-all-start = ((bf16[3,256,16,2,128]{4,2,3,0,1:T(8,128)(2,1)}), bf16[3,256,16,2,128]{4,2,3,0,1:T(8,128)(2,1)}, u32[]{:S(2)}, u32[]{:S(2)}) async-start(bf16[3,256,16,2,128]{4,2,3,0,1:T(8,128)(2,1)} %copy.75), calls=%async_computation | async-start | bytes 12582912 | tf_op jit(solution)/shard_map/all_to_all | solution.py:53
  47.3 91.2 %all-gather.6.cloned.1.call-done = s32[8,32768,1]{1,0,2:T(8,128)} async-done(((s32[8,512,1]{1,0,2:T(8,128)}), s32[8,32768,1]{1,0,2:T(8,128)}) %all-gather.6.cloned.1.call-update) | async-done | bytes 1048592 | tf_op jit(solution)/shard_map/all_gather | solution.py:56
  138.5 1.4 copy.64
  141.2 56.2 %all-to-all-done = bf16[3,256,16,2,128]{4,2,3,0,1:T(8,128)(2,1)} async-done(((bf16[3,256,16,2,128]{4,2,3,0,1:T(8,128)(2,1)}), bf16[3,256,16,2,128]{4,2,3,0,1:T(8,128)(2,1)}, u32[]{:S(2)}, u32[]{:S(2)}) %all-to-all-start) | async-done | bytes 6291488 | tf_op jit(solution)/shard_map/all_to_all | solution.py:53
  197.4 4.5 %fusion.45 = (bf16[1,16,256,2,128]{4,1,3,0,2:T(8,128)(2,1)S(1)}, bf16[1,16,256,2,128]{4,1,3,0,2:T(8,128)(2,1)S(1)}, bf16[1,16,256,2,128]{4,1,3,0,2:T(8,128)(2,1)S(1)}) fusion(bf16[3,16,256,2,128]{4,1,3,0,2:T(8,128)(2,1)} %bitcast.17), kind=kLoop, calls=%fused_computation.60 | loop fusion | bytes 12582912 | tf_op jit(solution)/shard_map/slice | solution.py:23
  201.9 2.0 copy.76
  203.9 3.2 copy.77
  207.2 3.2 copy.78
  210.4 9.8 %fusion.46 = (f32[16,512]{1,0:T(8,128)S(1)}, f32[16,512,512]{1,2,0:T(8,128)}) fusion(pred[16,512]{1,0:T(8,128)(4,1)S(1)} %copy.66, bf16[16,512,128]{2,1,0:T(8,128)(2,1)S(1)} %bitcast.71, bf16[16,512,128]{2,1,0:T(8,128)(2,1)} %bitcast.72), kind=kOutput, calls=%fused_computation.61 | convolution fusion | flops 1090519552 | bytes 21012480 | tf_op jit(solution)/shard_map/sub | solution.py:27
  220.2 9.3 %convert_bitcast_fusion.1 = bf16[16,64,8,128]{3,2,1,0:T(8,128)(2,1)S(1)} fusion(bf16[16,512,128]{2,1,0:T(8,128)(2,1)} %bitcast.73, f32[16,512,512]{1,2,0:T(8,128)} %get-tuple-element.11, f32[16,512]{1,0:T(8,128)S(1)} %get-tuple-element.10), kind=kOutput, calls=%fused_computation.28 | convolution fusion | flops 1083179008 | bytes 21004288 | tf_op jit(solution)/shard_map/cqk,ckd->cqd/dot_general | solution.py:29
  229.5 3.8 %copy.80 = bf16[16,64,8,128]{3,0,2,1:T(8,128)(2,1)} copy(bf16[16,64,8,128]{3,2,1,0:T(8,128)(2,1)S(1)} %convert_bitcast_fusion.1) | data formatting | bytes 4194304 | tf_op jit(solution)/shard_map/reshape | solution.py:66
  233.3 5.4 %all-to-all-start.1 = ((bf16[16,64,8,128]{3,0,2,1:T(8,128)(2,1)}), bf16[16,64,8,128]{3,0,2,1:T(8,128)(2,1)S(1)}, u32[]{:S(2)}, u32[]{:S(2)}) async-start(bf16[16,64,8,128]{3,0,2,1:T(8,128)(2,1)} %copy.80), calls=%async_computation.1 | async-start | bytes 4194304 | tf_op jit(solution)/shard_map/all_to_all | solution.py:67
  239.0 1.6 copy.82
  241.3 48.7 %all-to-all-done.1 = bf16[16,64,8,128]{3,0,2,1:T(8,128)(2,1)S(1)} async-done(((bf16[16,64,8,128]{3,0,2,1:T(8,128)(2,1)}), bf16[16,64,8,128]{3,0,2,1:T(8,128)(2,1)S(1)}, u32[]{:S(2)}, u32[]{:S(2)}) %all-to-all-start.1) | async-done | bytes 2097184 | tf_op jit(solution)/shard_map/all_to_all | solution.py:67
  290.1 1.4 copy.81
  291.4 2.6 fusion.25
  294.8 9.5 %convolution_convert_fusion = bf16[512,4096]{1,0:T(8,128)(2,1)} fusion(bf16[1024,4096]{0,1:T(8,128)(2,1)} %all-gather.4.cloned.1.call-done, bf16[64,8,8,128]{3,2,1,0:T(8,128)(2,1)S(1)} %bitcast.77), kind=kOutput, calls=%fused_computation.10 | convolution fusion | flops 4297064448 | bytes 13631488 | tf_op jit(solution)/shard_map/dot_general | solution.py:75
  304.3 43.5 %reduce-scatter.2.cloned.1.call-done = bf16[512,1024]{1,0:T(8,128)(2,1)} async-done(((bf16[512,4096]{1,0:T(8,128)(2,1)}), bf16[512,1024]{1,0:T(8,128)(2,1)}) %reduce-scatter.2.cloned.1.call-update) | async-done | bytes 1048592 | tf_op jit(solution)/shard_map/reduce_scatter | solution.py:80
  (50 shorter events, 10.6 us)
Async XLA Ops:
  6.5 0.8 copy-start
  6.5 2.8 copy-start.2
  9.4 2.0 copy-start.3
  11.4 2.0 copy-start.4
  13.4 2.0 copy-start.5
  14.0 1.3 copy-start.7
  29.1 168.3 %all-to-all-start = ((bf16[3,256,16,2,128]{4,2,3,0,1:T(8,128)(2,1)}), bf16[3,256,16,2,128]{4,2,3,0,1:T(8,128)(2,1)}, u32[]{:S(2)}, u32[]{:S(2)}) async-start(bf16[3,256,16,2,128]{4,2,3,0,1:T(8,128)(2,1)} %copy.75), calls=%async_computation | async-start | bytes 12582912 | tf_op jit(solution)/shard_map/all_to_all | solution.py:53
  45.6 92.9 %all-gather.6.cloned.1.call-start = ((), (), s32[]{:S(2)}) async-start(), calls=%async_computation.5 | async-start | bytes 1064960 | tf_op jit(solution)/shard_map/all_gather | solution.py:56
  46.4 248.4 %all-gather.4.cloned.1.call-start = ((), (), s32[]{:S(2)}) async-start(), calls=%async_computation.3 | async-start | bytes 8519680 | tf_op jit(solution)/shard_map/all_gather | solution.py:77
  233.3 5.5 %copy-start.8 = (s32[8,512,1]{1,0,2:T(8,128)S(1)}, s32[8,512,1]{1,0,2:T(8,128)}, u32[]{:S(2)}) copy-start(s32[8,512,1]{1,0,2:T(8,128)} %copy.105) | copy-start | bytes 49156
  233.3 56.8 %all-to-all-start.1 = ((bf16[16,64,8,128]{3,0,2,1:T(8,128)(2,1)}), bf16[16,64,8,128]{3,0,2,1:T(8,128)(2,1)S(1)}, u32[]{:S(2)}, u32[]{:S(2)}) async-start(bf16[16,64,8,128]{3,0,2,1:T(8,128)(2,1)} %copy.80), calls=%async_computation.1 | async-start | bytes 4194304 | tf_op jit(solution)/shard_map/all_to_all | solution.py:67
  238.7 109.1 %reduce-scatter.2.cloned.1.call-start = ((), (), s32[]{:S(2)}) async-start(), calls=%async_computation.4 | async-start | bytes 5242880 | tf_op jit(solution)/shard_map/reduce_scatter | solution.py:80
  241.3 50.1 %copy-start.6 = (bf16[8,4,128,128]{3,2,0,1:T(8,128)(2,1)S(1)}, bf16[8,4,128,128]{3,2,0,1:T(8,128)(2,1)}, u32[]{:S(2)}) copy-start(bf16[8,4,128,128]{3,2,0,1:T(8,128)(2,1)} %copy.82) | copy-start | bytes 3145732
  304.3 43.6 %copy-start.1 = (s32[32,512,1]{1,2,0:T(1,128)S(1)}, s32[32,512,1]{1,2,0:T(1,128)}, u32[]{:S(2)}) copy-start(s32[32,512,1]{1,2,0:T(1,128)} %param.8) | copy-start | bytes 196612
Sparse Core Ops, SparseCore 0:
  49.3 89.2 all-gather.5
  141.3 91.9 all-gather.3
  304.4 43.3 reduce-scatter.1
where the time goes:
time: 355 us; the launch traced here: 354 us
  waiting for transfers between devices  241 us (68%)
  local copies, waits for them, and re-layouts  40.2 us (11%)
  matrix products  35.8 us (10%)
  starting transfers between devices  22.1 us (6%)
  between operations  13.4 us (4%)
    all_gather x1, waiting for transfers between devices, body(): seen_ids = lax.all_gather(group_ids, 'seq', axis=1, tiled=True)  91.2 us
    all_to_all x1, waiting for transfers between devices, body(): lax.all_to_all(packed, ('seq', 'head'), split_axis=1, concat_axis=1, tile...  56.2 us
    all_to_all x1, waiting for transfers between devices, body(): lax.all_to_all(result_block, 'seq', split_axis=1, concat_axis=1, tiled=True)  48.7 us
    reduce_scatter x1, waiting for transfers between devices, body(): lax.psum_scatter(partial_value.astype(jnp.bfloat16), 'head', scatter_dime...  43.5 us
    all_to_all x1, starting transfers between devices, body(): lax.all_to_all(packed, ('seq', 'head'), split_axis=1, concat_axis=1, tile...  16.5 us
    sub x1, matrix products, attend_blocks(): raised = jnp.exp(scores - row_max)  9.82 us
    dot_general x1, matrix products, body(): jnp.dot(gathered, lax.all_gather(out_weight, 'seq', axis=1, tiled=True),...  9.5 us
    dot_general x1, matrix products, attend_blocks(): jnp.einsum('cqk,ckd->cqd', weights, packed[2], preferred_element_type=jnp...  9.25 us
  transfers between devices with their start and end apart: 5, of which 4 were waited for; matrix products, arithmetic and copies ran while one was open for 13% of the time, Pallas kernels for 0%

commit v1 on v0

--- a/solution.py
+++ b/solution.py
@@ -6,6 +6,13 @@
 HEADS = 32
 HD = 128
 CLUSTERS = 128
+
+
+def exchange_gather(x, name, d):
+    size = lax.axis_size(name)
+    blocks = jnp.stack([x for _ in range(size)])
+    blocks = lax.all_to_all(blocks, name, split_axis=0, concat_axis=0)
+    return jnp.concatenate(blocks, axis=d)
 
 
 def slot_table(block_ids, slot_depth):
@@ -53,7 +60,7 @@
     arrived = lax.all_to_all(packed, ("seq", "head"), split_axis=1, concat_axis=1, tiled=True)
     arrived = arrived.transpose(0, 2, 1, 3, 4).reshape(3, per_owner, n_src * slot_depth, HD)
     group_ids = lax.dynamic_slice_in_dim(all_ids, head_group * group_heads, group_heads, 0)
-    seen_ids = lax.all_gather(group_ids, "seq", axis=1, tiled=True)
+    seen_ids = exchange_gather(group_ids, "seq", 1)
     seen_ids = seen_ids.reshape(group_heads, n_src, sub_rows)
     owned = jnp.arange(CLUSTERS // n_seq, dtype=jnp.int32) * n_seq + lax.axis_index("seq")
     counts = jnp.sum(

time: 355 us -> 385 us (1.085)
  waiting for transfers between devices: 241 us -> 267 us
  starting transfers between devices: 22.1 us -> 28 us
    all_to_all x1, waiting for transfers between devices: 56.2 us -> 166 us  [body(): lax.all_to_all(packed, ('seq', 'head'), split_axis=1, concat_axis=1, tile...]
    all_gather x1 -> x0, waiting for transfers between devices: 91.2 us -> none  [body(): seen_ids = lax.all_gather(group_ids, 'seq', axis=1, tiled=True)]
    all_to_all x0 -> x1, starting transfers between devices: none -> 13.2 us  [exchange_gather(): blocks = lax.all_to_all(blocks, name, split_axis=0, concat_axis=0)]
    all_to_all x0 -> x1, waiting for transfers between devices: none -> 8.32 us  [exchange_gather(): blocks = lax.all_to_all(blocks, name, split_axis=0, concat_axis=0)]
    all_to_all x1, starting transfers between devices: 16.5 us -> 9.57 us  [body(): lax.all_to_all(packed, ('seq', 'head'), split_axis=1, concat_axis=1, tile...]
  transfers between devices with their start and end apart: 5 -> 5, of which waited for: 4 -> 4; matrix products, arithmetic and copies ran while one was open for 13% -> 17% of each run, Pallas kernels for 0% -> 0%
where the time goes in v1:
time: 385 us; the launch traced here: 384 us
  waiting for transfers between devices  267 us (69%)
  local copies, waits for them, and re-layouts  40.4 us (10%)
  matrix products  34.1 us (9%)
  starting transfers between devices  28 us (7%)
  between operations  13.7 us (4%)
    all_to_all x1, waiting for transfers between devices, body(): lax.all_to_all(packed, ('seq', 'head'), split_axis=1, concat_axis=1, tile...  166 us
    all_to_all x1, waiting for transfers between devices, body(): lax.all_to_all(result_block, 'seq', split_axis=1, concat_axis=1, tiled=True)  48.8 us
    reduce_scatter x1, waiting for transfers between devices, body(): lax.psum_scatter(partial_value.astype(jnp.bfloat16), 'head', scatter_dime...  43.6 us
    all_to_all x1, starting transfers between devices, exchange_gather(): blocks = lax.all_to_all(blocks, name, split_axis=0, concat_axis=0)  13.2 us
    sub x1, matrix products, attend_blocks(): raised = jnp.exp(scores - row_max)  9.84 us
    all_to_all x1, starting transfers between devices, body(): lax.all_to_all(packed, ('seq', 'head'), split_axis=1, concat_axis=1, tile...  9.57 us
    dot_general x1, matrix products, body(): jnp.dot(gathered, lax.all_gather(out_weight, 'seq', axis=1, tiled=True),...  9.48 us
    dot_general x1, matrix products, attend_blocks(): jnp.einsum('cqk,ckd->cqd', weights, packed[2], preferred_element_type=jnp...  8.89 us
  transfers between devices with their start and end apart: 5, of which 4 were waited for; matrix products, arithmetic and copies ran while one was open for 17% of the time, Pallas kernels for 0%

profile of v1, /device:TPU:1, one launch (start us, length us, event | category | flops | bytes accessed | tf_op | source)
XLA Modules:
  0.0 384.5 jit_solution(870826962583269959)
XLA Ops:
  8.5 13.2 %all-to-all-start = ((s32[64,8,512]{2,1,0:T(8,128)}), s32[64,8,512]{2,1,0:T(8,128)S(1)}, u32[]{:S(2)}, u32[]{:S(2)}) async-start(s32[64,8,512]{2,1,0:T(8,128)} %stack.7), calls=%async_computation | async-start | bytes 2097152 | tf_op jit(solution)/shard_map/all_to_all | solution.py:14
  22.4 1.3 copy.68
  26.3 1.3 copy.70
  29.5 2.0 convert_bitcast_fusion
  31.5 2.6 copy.71
  34.1 4.0 %copy.72 = bf16[3,64,4,16,2,128]{5,3,4,2,1,0:T(8,128)(2,1)S(1)} copy(bf16[3,64,4,16,2,128]{5,1,3,2,4,0:T(8,128)(2,1)S(1)} %bitcast.68) | data formatting | bytes 12582912 | tf_op jit(solution)/shard_map/transpose | solution.py:59
  38.2 3.7 copy.73
  41.9 8.3 %all-to-all-done = s32[64,8,512]{2,1,0:T(8,128)S(1)} async-done(((s32[64,8,512]{2,1,0:T(8,128)}), s32[64,8,512]{2,1,0:T(8,128)S(1)}, u32[]{:S(2)}, u32[]{:S(2)}) %all-to-all-start) | async-done | bytes 1048608 | tf_op jit(solution)/shard_map/all_to_all | solution.py:14
  50.2 9.6 %all-to-all-start.1 = ((bf16[3,256,16,2,128]{4,2,3,0,1:T(8,128)(2,1)}), bf16[3,256,16,2,128]{4,2,3,0,1:T(8,128)(2,1)}, u32[]{:S(2)}, u32[]{:S(2)}) async-start(bf16[3,256,16,2,128]{4,2,3,0,1:T(8,128)(2,1)} %copy.73), calls=%async_computation.1 | async-start | bytes 12582912 | tf_op jit(solution)/shard_map/all_to_all | solution.py:60
  62.6 165.5 %all-to-all-done.1 = bf16[3,256,16,2,128]{4,2,3,0,1:T(8,128)(2,1)} async-done(((bf16[3,256,16,2,128]{4,2,3,0,1:T(8,128)(2,1)}), bf16[3,256,16,2,128]{4,2,3,0,1:T(8,128)(2,1)}, u32[]{:S(2)}, u32[]{:S(2)}) %all-to-all-start.1) | async-done | bytes 6291488 | tf_op jit(solution)/shard_map/all_to_all | solution.py:60
  228.1 4.2 %fusion.45 = (bf16[1,16,256,2,128]{4,1,3,0,2:T(8,128)(2,1)S(1)}, bf16[1,16,256,2,128]{4,1,3,0,2:T(8,128)(2,1)S(1)}, bf16[1,16,256,2,128]{4,1,3,0,2:T(8,128)(2,1)S(1)}) fusion(bf16[3,16,256,2,128]{4,1,3,0,2:T(8,128)(2,1)} %bitcast.18), kind=kLoop, calls=%fused_computation.61 | loop fusion | bytes 12582912 | tf_op jit(solution)/shard_map/slice | solution.py:30
  232.3 2.0 copy.74
  234.3 3.2 copy.75
  237.5 3.3 copy.76
  240.8 9.8 %fusion.46 = (f32[16,512]{1,0:T(8,128)S(1)}, f32[16,512,512]{1,2,0:T(8,128)}) fusion(pred[16,512]{1,0:T(8,128)(4,1)S(1)} %copy.64, bf16[16,512,128]{2,1,0:T(8,128)(2,1)S(1)} %bitcast.74, bf16[16,512,128]{2,1,0:T(8,128)(2,1)} %bitcast.75), kind=kOutput, calls=%fused_computation.62 | convolution fusion | flops 1090519552 | bytes 21012480 | tf_op jit(solution)/shard_map/sub | solution.py:34
  250.6 8.9 %convert_bitcast_fusion.1 = bf16[16,64,8,128]{3,2,1,0:T(8,128)(2,1)S(1)} fusion(bf16[16,512,128]{2,1,0:T(8,128)(2,1)} %bitcast.76, f32[16,512,512]{1,2,0:T(8,128)} %get-tuple-element.11, f32[16,512]{1,0:T(8,128)S(1)} %get-tuple-element.10), kind=kOutput, calls=%fused_computation.28 | convolution fusion | flops 1083179008 | bytes 21004288 | tf_op jit(solution)/shard_map/cqk,ckd->cqd/dot_general | solution.py:36
  259.5 3.8 copy.78
  263.3 5.2 %all-to-all-start.2 = ((bf16[16,64,8,128]{3,0,2,1:T(8,128)(2,1)}), bf16[16,64,8,128]{3,0,2,1:T(8,128)(2,1)S(1)}, u32[]{:S(2)}, u32[]{:S(2)}) async-start(bf16[16,64,8,128]{3,0,2,1:T(8,128)(2,1)} %copy.78), calls=%async_computation.2 | async-start | bytes 4194304 | tf_op jit(solution)/shard_map/all_to_all | solution.py:74
  268.8 1.6 copy.80
  271.1 48.8 %all-to-all-done.2 = bf16[16,64,8,128]{3,0,2,1:T(8,128)(2,1)S(1)} async-done(((bf16[16,64,8,128]{3,0,2,1:T(8,128)(2,1)}), bf16[16,64,8,128]{3,0,2,1:T(8,128)(2,1)S(1)}, u32[]{:S(2)}, u32[]{:S(2)}) %all-to-all-start.2) | async-done | bytes 2097184 | tf_op jit(solution)/shard_map/all_to_all | solution.py:74
  319.9 1.4 copy.79
  321.2 2.6 fusion.25
  324.6 9.5 %convolution_convert_fusion = bf16[512,4096]{1,0:T(8,128)(2,1)} fusion(bf16[1024,4096]{0,1:T(8,128)(2,1)} %all-gather.2.cloned.1.call-done, bf16[64,8,8,128]{3,2,1,0:T(8,128)(2,1)S(1)} %bitcast.79), kind=kOutput, calls=%fused_computation.10 | convolution fusion | flops 4297064448 | bytes 13631488 | tf_op jit(solution)/shard_map/dot_general | solution.py:82
  334.1 43.6 %reduce-scatter.2.cloned.1.call-done = bf16[512,1024]{1,0:T(8,128)(2,1)} async-done(((bf16[512,4096]{1,0:T(8,128)(2,1)}), bf16[512,1024]{1,0:T(8,128)(2,1)}) %reduce-scatter.2.cloned.1.call-update) | async-done | bytes 1048592 | tf_op jit(solution)/shard_map/reduce_scatter | solution.py:87
  (51 shorter events, 11.5 us)
Async XLA Ops:
  6.5 0.8 copy-start
  6.5 15.1 %copy-start.2 = (bf16[128,4096]{1,0:T(8,128)(2,1)S(1)}, bf16[128,4096]{1,0:T(8,128)(2,1)}, u32[]{:S(2)}) copy-start(bf16[128,4096]{1,0:T(8,128)(2,1)} %param.5) | copy-start | bytes 3145732
  8.5 41.7 %all-to-all-start = ((s32[64,8,512]{2,1,0:T(8,128)}), s32[64,8,512]{2,1,0:T(8,128)S(1)}, u32[]{:S(2)}, u32[]{:S(2)}) async-start(s32[64,8,512]{2,1,0:T(8,128)} %stack.7), calls=%async_computation | async-start | bytes 2097152 | tf_op jit(solution)/shard_map/all_to_all | solution.py:14
  22.4 1.3 copy-start.3
  24.4 1.3 copy-start.4
  27.7 1.2 copy-start.5
  27.7 1.5 copy-start.6
  27.7 1.9 copy-start.7
  50.2 177.9 %all-to-all-start.1 = ((bf16[3,256,16,2,128]{4,2,3,0,1:T(8,128)(2,1)}), bf16[3,256,16,2,128]{4,2,3,0,1:T(8,128)(2,1)}, u32[]{:S(2)}, u32[]{:S(2)}) async-start(bf16[3,256,16,2,128]{4,2,3,0,1:T(8,128)(2,1)} %copy.73), calls=%async_computation.1 | async-start | bytes 12582912 | tf_op jit(solution)/shard_map/all_to_all | solution.py:60
  59.8 264.8 %all-gather.2.cloned.1.call-start = ((), (), s32[]{:S(2)}) async-start(), calls=%async_computation.4 | async-start | bytes 8519680 | tf_op jit(solution)/shard_map/all_gather | solution.py:84
  263.3 56.6 %all-to-all-start.2 = ((bf16[16,64,8,128]{3,0,2,1:T(8,128)(2,1)}), bf16[16,64,8,128]{3,0,2,1:T(8,128)(2,1)S(1)}, u32[]{:S(2)}, u32[]{:S(2)}) async-start(bf16[16,64,8,128]{3,0,2,1:T(8,128)(2,1)} %copy.78), calls=%async_computation.2 | async-start | bytes 4194304 | tf_op jit(solution)/shard_map/all_to_all | solution.py:74
  268.5 109.1 %reduce-scatter.2.cloned.1.call-start = ((), (), s32[]{:S(2)}) async-start(), calls=%async_computation.5 | async-start | bytes 5242880 | tf_op jit(solution)/shard_map/reduce_scatter | solution.py:87
  271.1 50.1 %copy-start.8 = (bf16[8,4,128,128]{3,2,0,1:T(8,128)(2,1)S(1)}, bf16[8,4,128,128]{3,2,0,1:T(8,128)(2,1)}, u32[]{:S(2)}) copy-start(bf16[8,4,128,128]{3,2,0,1:T(8,128)(2,1)} %copy.80) | copy-start | bytes 3145732
  334.0 43.6 %copy-start.1 = (s32[32,512,1]{1,2,0:T(1,128)S(1)}, s32[32,512,1]{1,2,0:T(1,128)}, u32[]{:S(2)}) copy-start(s32[32,512,1]{1,2,0:T(1,128)} %param.8) | copy-start | bytes 196612
Sparse Core Ops, SparseCore 0:
  63.4 139.8 all-gather.1
  334.2 43.4 reduce-scatter.1
